TPU v7x, 512 devices: a whole 4x4x16 slice. The times are simulated.
512 devices in a mesh: band: 16 (over x, y), lon: 32 (over z, core).
Axes of the slice: x: 4, y: 4, z: 16, core: 2. Of those that a mesh axis runs over, the one named last changes fastest.
Arguments:
- sky_maps: float32 [16, 8192, 256], P(None, ('band', 'lon')), may hold values from -9 to 9
- noise_var: float32 [8192, 256], P(('band', 'lon')), may hold values from 1 to 4
- position: float32 [3, 8192, 256], P(None, ('band', 'lon')), may hold values from -1 to 1
- leaf_basis: float32 [8192, 256, 64], P(('band', 'lon')), may hold values from -1 to 1
- leaf_couple: float32 [8192, 4, 64, 64], P(('band', 'lon')), as said below
- transfer: float32 [8192, 64, 64], P(('band', 'lon')), may hold values from -2 to 2
- panel_couple: float32 [1024, 2, 64, 64], P(('band', 'lon')), as said below
- near_list: int32 [8192, 5], P(('band', 'lon')), may hold values from -1 to 8191, as said below
- far_list: int32 [8192, 4], P(('band', 'lon')), may hold values from 0 to 8191, as said below
- panel_list: int32 [1024, 2], P(('band', 'lon')), may hold values from 0 to 1023, as said below
- leaf_panel: int32 [8192], P(('band', 'lon')), may hold values from 0 to 1
Outputs:
- solution: float32 [16, 8192, 256], P(None, ('band', 'lon'))
- residual: float32 [16, 8192, 256], P(None, ('band', 'lon'))
Inputs may be any that keep to these rules, and one draw needn't show every extreme that they name: `near_list`: entry 0 of a row is the leaf itself; the entries after it that are not -1 come first and are distinct leaves of the same band at cycle distance 1 or 2, the cycle closing; leaf j stands in leaf i's row exactly when i stands in j's. `far_list`: distinct leaves of the same band at cycle distance 3 to 6, the cycle closing; leaf j stands in leaf i's row exactly when i stands in j's. If leaf j stands in slot s of far_list[i] and leaf i in slot t of far_list[j], then leaf_couple[j, t] is the transpose of leaf_couple[i, s]. `panel_list`: entries are panel s of sectors of other bands at the same longitude (sector ids differing by a nonzero multiple of the sectors of a band), s being the panel's own index in its sector; panel j stands in panel k's row as often as k stands in j's. If panel j stands in slot s of panel_list[k] and these slots pair up with the slots t of panel_list[j] that hold k, then panel_couple[j, t] is the transpose of panel_couple[k, s].
All inputs are finite; a program needn't handle non-finite values.
Results may differ from a plain program's by a relative error of at most 0.0003.
Values sent between devices are 32-bit elements; how exact they have to be, the bound alone decides.
No kernel may reach another device: no remote copies, remote signals or barrier semaphores. Data moves between devices by JAX's collectives and lax.ppermute only.
A program may use at most 128 MiB of HBM per device.

v0:
```python
import math
import jax
import jax.numpy as jnp
from jax import lax
from jax.sharding import PartitionSpec as P

REACH = 6
ITERS = 2
HIGHEST_PRECISION = lax.Precision.HIGHEST
ROOT_THREE = math.sqrt(3.0)
AMPLITUDE = 0.02


def extended(cells, sides, width):
    for axis, dim in sides:
        count = lax.axis_size(axis)
        head = lax.slice_in_dim(cells, 0, width, axis=dim)
        tail = lax.slice_in_dim(cells, cells.shape[dim] - width, cells.shape[dim], axis=dim)
        cells = jnp.concatenate(
            [
                lax.ppermute(tail, axis, [(i, (i + 1) % count) for i in range(count)]),
                cells,
                lax.ppermute(head, axis, [((i + 1) % count, i) for i in range(count)]),
            ],
            axis=dim,
        )
    return cells


def all_sum(vector, axes):
    for axis in axes:
        count = lax.axis_size(axis)
        if count & count - 1:
            vector = lax.psum(vector, axis)
            continue
        stride = 1
        while stride < count:
            vector = vector + lax.ppermute(vector, axis, [(i, i ^ stride) for i in range(count)])
            stride *= 2
    return vector


def matern_block(rows_pos, cols_pos, length_scale):
    squared = jnp.zeros((cols_pos.shape[1], rows_pos.shape[1], cols_pos.shape[2]), jnp.float32)
    for component in range(3):
        offset = rows_pos[component][None, :, None] - cols_pos[component][:, None, :]
        squared = squared + offset * offset
    scaled = ROOT_THREE * jnp.sqrt(squared) / length_scale
    return AMPLITUDE * (1.0 + scaled) * jnp.exp(-scaled)


def on_device(
    sky_maps,
    noise_var,
    position,
    leaf_basis,
    leaf_couple,
    transfer,
    panel_couple,
    near_list,
    far_list,
    panel_list,
    leaf_panel,
):
    lon_index = lax.axis_index("lon")
    lon_count = lax.axis_size("lon")
    local_leaves = sky_maps.shape[1]
    pixel_count = sky_maps.shape[2]
    cycle_size = local_leaves * lon_count
    panel_count = panel_couple.shape[0]
    length_scale = 2.0 * math.pi / cycle_size
    first_leaf = lon_index * local_leaves
    near_depth = 2

    def rim_index(leaf_ids, depth):
        return (leaf_ids % cycle_size - first_leaf + depth) % cycle_size

    near_valid = near_list >= 0
    near_rows = rim_index(jnp.where(near_valid, near_list, near_list[:, :1]), near_depth)
    far_rows = rim_index(far_list, REACH)
    rim_pos = extended(position, (("lon", 1),), near_depth)

    def leaf_blocks(inputs):
        rows_pos, rows_index, slot_mask = inputs
        cols_pos = rim_pos[:, rows_index]
        return matern_block(rows_pos, cols_pos, length_scale) * slot_mask[:, None, None]

    near_blocks = jax.vmap(lambda *leaf: leaf_blocks(leaf))(
        jnp.transpose(position, (1, 0, 2)), near_rows, near_valid.astype(jnp.float32)
    )
    band_slot = panel_list // (lon_count * panel_count)
    gathered_rows = band_slot * panel_count + panel_list % panel_count
    membership = (leaf_panel[:, None] == jnp.arange(panel_count, dtype=jnp.int32)[None, :]).astype(
        jnp.float32
    )

    def square_total(vector):
        return all_sum(jnp.sum(vector * vector, axis=(1, 2)), ("lon", "band"))

    def covariance_apply(direction):
        coeffs = jnp.einsum("lpr,mlp->mlr", leaf_basis, direction, precision=HIGHEST_PRECISION)
        joined = jnp.concatenate([direction, coeffs], axis=2)
        rim_joined = extended(joined, (("lon", 1),), REACH)
        rim_values = rim_joined[
            :, REACH - near_depth : REACH + local_leaves + near_depth, :pixel_count
        ]
        rim_coeffs = rim_joined[:, :, pixel_count:]
        near_part = jnp.einsum(
            "lspq,mlsq->mlp", near_blocks, rim_values[:, near_rows], precision=HIGHEST_PRECISION
        )
        leaf_far = jnp.einsum(
            "lsab,mlsb->mla", leaf_couple, rim_coeffs[:, far_rows], precision=HIGHEST_PRECISION
        )
        upward = jnp.einsum("lab,mla->mlb", transfer, coeffs, precision=HIGHEST_PRECISION)
        panel_coeffs = jnp.einsum("lk,mlb->mkb", membership, upward, precision=HIGHEST_PRECISION)
        band_coeffs = lax.all_gather(panel_coeffs, "band", axis=1, tiled=True)
        panel_far = jnp.einsum(
            "ksab,mksb->mka",
            panel_couple,
            band_coeffs[:, gathered_rows],
            precision=HIGHEST_PRECISION,
        )
        downward = jnp.einsum("lk,mkb->mlb", membership, panel_far, precision=HIGHEST_PRECISION)
        leaf_far = leaf_far + jnp.einsum(
            "lab,mlb->mla", transfer, downward, precision=HIGHEST_PRECISION
        )
        far_part = jnp.einsum("lpr,mlr->mlp", leaf_basis, leaf_far, precision=HIGHEST_PRECISION)
        return noise_var[None] * direction + near_part + far_part

    solution = jnp.zeros_like(sky_maps)
    residual = sky_maps
    direction = sky_maps
    norm_now = square_total(residual)
    applied = covariance_apply(direction)
    for iteration in range(ITERS):
        curvature_sum = all_sum(jnp.sum(direction * applied, axis=(1, 2)), ("lon", "band"))
        step_size = norm_now / curvature_sum
        solution = solution + step_size[:, None, None] * direction
        residual = residual - step_size[:, None, None] * applied
        if iteration + 1 < ITERS:
            norm_next = square_total(residual)
            applied_residual = covariance_apply(residual)
            ratio = (norm_next / norm_now)[:, None, None]
            direction = residual + ratio * direction
            applied = applied_residual + ratio * applied
            norm_now = norm_next
    return (solution, residual)


def solution(mesh):
    placed = (
        P(None, ("band", "lon"), None),
        P(("band", "lon"), None),
        P(None, ("band", "lon"), None),
        P(("band", "lon"), None, None),
        P(("band", "lon"), None, None, None),
        P(("band", "lon"), None, None),
        P(("band", "lon"), None, None, None),
        P(("band", "lon"), None),
        P(("band", "lon"), None),
        P(("band", "lon"), None),
        P(("band", "lon")),
    )
    return jax.shard_map(
        on_device,
        mesh=mesh,
        in_specs=placed,
        out_specs=(P(None, ("band", "lon"), None), P(None, ("band", "lon"), None)),
        check_vma=False,
    )
```

profile of v0, /device:TPU:32, one launch (start us, length us, event | category | flops | bytes accessed | tf_op | source)
XLA Modules:
  0.0 391.8 jit_solution(15250787226746953187)
XLA Ops:
  2.5 1.9 collective-permute-start
  6.4 5.1 %collective-permute-start.12 = (f32[3,2,256]{2,0,1:T(4,128)}, f32[3,2,256]{2,0,1:T(4,128)}, u32[]{:S(2)}, u32[]{:S(2)}) collective-permute-start(f32[3,2,256]{2,0,1:T(4,128)} %get-tuple-element.24), channel_id=1, source_target_pairs={{1,0},{2,1},{3,2},{4,3},{5,4},{6,5},{7,6},{8,7},{9,8},{10,9},{11,1... | collective-permute-start | bytes 18440 | tf_op jit(solution)/shard_map/ppermute | solution.py:23
  12.6 2.4 convolution_bitcast_fusion.9
  21.0 20.7 %all_gather.6 = f32[16,32,64]{2,0,1:T(8,128)S(1)} all-gather(f32[16,2,64]{2,0,1:T(8,128)S(1)} %copy.55), channel_id=1, replica_groups=mesh['band'=16,'lon'=32] {'band'}, dimensions={1}, use_global_device_ids=true | all-gather | bytes 139264 | tf_op jit(solution)/shard_map/all_gather | solution.py:116
  44.9 10.6 %collective-permute-start.1 = (f32[16]{0:T(128)S(1)}, f32[16]{0:T(128)S(1)}, u32[]{:S(2)}, u32[]{:S(2)}) collective-permute-start(f32[16]{0:T(128)S(1)} %add.208), channel_id=1, source_target_pairs={{0,2},{1,3},{2,0},{3,1},{4,6},{5,7},{6,4},{7,5},{8,10},{9,11},{10,... | collective-permute-start | bytes 200 | tf_op jit(solution)/shard_map/ppermute | solution.py:38
  59.5 3.8 collective-permute-done.2
  63.3 2.5 collective-permute-start.3
  67.1 5.5 %collective-permute-done.3 = f32[16]{0:T(128)S(1)} collective-permute-done((f32[16]{0:T(128)S(1)}, f32[16]{0:T(128)S(1)}, u32[]{:S(2)}, u32[]{:S(2)}) %collective-permute-start.3) | collective-permute-done | bytes 96 | tf_op jit(solution)/shard_map/ppermute | solution.py:38
  73.2 9.1 %collective-permute-start.4 = (f32[16]{0:T(128)}, f32[16]{0:T(128)}, u32[]{:S(2)}, u32[]{:S(2)}) collective-permute-start(f32[16]{0:T(128)} %add.211), channel_id=1, source_target_pairs={{0,16},{1,17},{2,18},{3,19},{4,20},{5,21},{6,22},{7,23},{8,24},{9,... | collective-permute-start | bytes 200 | tf_op jit(solution)/shard_map/ppermute | solution.py:38
  90.0 3.0 convolution_bitcast_fusion.7
  94.0 32.2 %fusion.27 = f32[16,16,256]{2,0,1:T(8,128)S(1)} fusion(f32[16,16,5,256]{3,0,2,1:T(8,128)S(1)} %bitcast.127, f32[16,5]{1,0:T(8,128)S(1)} %copy-done.39, f32[16,5,256]{2,1,0:T(8,128)S(1)} %copy-done.26, f32[16,256]{1,0:T(8,128)S(1)} %copy-done.32, f32[16,5,256]{2,1,0:T(8,128)S(1)} %copy-done.25, f32[16,256]{1,0:T(8,128)S(1)} %copy-done.34, ...), kind=kOutput, calls=%fused_computation.37 | convolution fusion | flops 1080164352 | bytes 2146624 | tf_op jit(solution)/shard_map/lspq,mlsq->mlp/dot_general | solution.py:108
  127.1 1.9 collective-permute-start.13
  130.1 3.9 collective-permute-start.14
  134.1 3.1 collective-permute-start.5
  137.2 1.9 collective-permute-start.15
  139.5 4.0 %collective-permute-done.15 = f32[16]{0:T(128)S(1)} collective-permute-done((f32[16]{0:T(128)S(1)}, f32[16]{0:T(128)S(1)}, u32[]{:S(2)}, u32[]{:S(2)}) %collective-permute-start.15) | collective-permute-done | bytes 96 | tf_op jit(solution)/shard_map/ppermute | solution.py:38
  143.5 4.3 %collective-permute-start.16 = (f32[16]{0:T(128)S(1)}, f32[16]{0:T(128)S(1)}, u32[]{:S(2)}, u32[]{:S(2)}) collective-permute-start(f32[16]{0:T(128)S(1)} %add.240), channel_id=1, source_target_pairs={{0,8},{1,9},{2,10},{3,11},{4,12},{5,13},{6,14},{7,15},{8,0},{9,1},... | collective-permute-start | bytes 200 | tf_op jit(solution)/shard_map/ppermute | solution.py:38
  147.8 4.6 %collective-permute-start.6 = (f32[16]{0:T(128)S(1)}, f32[16]{0:T(128)S(1)}, u32[]{:S(2)}, u32[]{:S(2)}) collective-permute-start(f32[16]{0:T(128)S(1)} %add.213), channel_id=1, source_target_pairs={{0,64},{32,96},{64,0},{96,32},{128,192},{160,224},{192,128},{224,1... | collective-permute-start | bytes 200 | tf_op jit(solution)/shard_map/ppermute | solution.py:38
  152.9 5.5 %collective-permute-start.17 = (f32[16]{0:T(128)S(1)}, f32[16]{0:T(128)S(1)}, u32[]{:S(2)}, u32[]{:S(2)}) collective-permute-start(f32[16]{0:T(128)S(1)} %add.241), channel_id=1, source_target_pairs={{0,16},{1,17},{2,18},{3,19},{4,20},{5,21},{6,22},{7,23},{8,24},{9,... | collective-permute-start | bytes 200 | tf_op jit(solution)/shard_map/ppermute | solution.py:38
  158.4 8.6 %collective-permute-done.17 = f32[16]{0:T(128)S(1)} collective-permute-done((f32[16]{0:T(128)S(1)}, f32[16]{0:T(128)S(1)}, u32[]{:S(2)}, u32[]{:S(2)}) %collective-permute-start.17) | collective-permute-done | bytes 96 | tf_op jit(solution)/shard_map/ppermute | solution.py:38
  167.0 2.7 collective-permute-start.18
  169.7 3.1 collective-permute-start.7
  172.9 4.1 %collective-permute-start.19 = (f32[16]{0:T(128)S(1)}, f32[16]{0:T(128)S(1)}, u32[]{:S(2)}, u32[]{:S(2)}) collective-permute-start(f32[16]{0:T(128)S(1)} %add.243), channel_id=1, source_target_pairs={{0,64},{32,96},{64,0},{96,32},{128,192},{160,224},{192,128},{224,1... | collective-permute-start | bytes 200 | tf_op jit(solution)/shard_map/ppermute | solution.py:38
  177.0 2.8 collective-permute-done.19
  179.8 2.7 collective-permute-start.20
  182.6 4.6 %collective-permute-start.8 = (f32[16]{0:T(128)S(1)}, f32[16]{0:T(128)S(1)}, u32[]{:S(2)}, u32[]{:S(2)}) collective-permute-start(f32[16]{0:T(128)S(1)} %add.215), channel_id=1, source_target_pairs={{0,256},{32,288},{64,320},{96,352},{128,384},{160,416},{192,448},{... | collective-permute-start | bytes 200 | tf_op jit(solution)/shard_map/ppermute | solution.py:38
  187.2 2.8 collective-permute-start.21
  190.0 4.1 %collective-permute-done.21 = f32[16]{0:T(128)S(1)} collective-permute-done((f32[16]{0:T(128)S(1)}, f32[16]{0:T(128)S(1)}, u32[]{:S(2)}, u32[]{:S(2)}) %collective-permute-start.21) | collective-permute-done | bytes 96 | tf_op jit(solution)/shard_map/ppermute | solution.py:38
  194.9 1.9 collective-permute-start.22
  198.6 2.2 collective-permute-start.23
  200.8 3.2 collective-permute-done.23
  204.0 1.9 collective-permute-start.24
  206.0 24.0 %all_gather.7 = f32[16,32,64]{2,0,1:T(8,128)} all-gather(f32[16,2,64]{2,0,1:T(8,128)S(1)} %copy.63), channel_id=1, replica_groups=mesh['band'=16,'lon'=32] {'band'}, dimensions={1}, use_global_device_ids=true | all-gather | bytes 139264 | tf_op jit(solution)/shard_map/all_gather | solution.py:116
  229.9 4.6 %collective-permute-start.25 = (f32[16]{0:T(128)S(1)}, f32[16]{0:T(128)}, u32[]{:S(2)}, u32[]{:S(2)}) collective-permute-start(f32[16]{0:T(128)S(1)} %add.249), channel_id=1, source_target_pairs={{0,8},{1,9},{2,10},{3,11},{4,12},{5,13},{6,14},{7,15},{8,0},{9,1},... | collective-permute-start | bytes 200 | tf_op jit(solution)/shard_map/ppermute | solution.py:38
  234.5 2.2 gather_fusion.6
  236.8 2.5 collective-permute-done.25
  239.9 5.5 %collective-permute-start.26 = (f32[16]{0:T(128)S(1)}, f32[16]{0:T(128)S(1)}, u32[]{:S(2)}, u32[]{:S(2)}) collective-permute-start(f32[16]{0:T(128)S(1)} %add.250), channel_id=1, source_target_pairs={{0,16},{1,17},{2,18},{3,19},{4,20},{5,21},{6,22},{7,23},{8,24},{9,... | collective-permute-start | bytes 200 | tf_op jit(solution)/shard_map/ppermute | solution.py:38
  246.5 7.5 %collective-permute-done.26 = f32[16]{0:T(128)S(1)} collective-permute-done((f32[16]{0:T(128)S(1)}, f32[16]{0:T(128)S(1)}, u32[]{:S(2)}, u32[]{:S(2)}) %collective-permute-start.26) | collective-permute-done | bytes 96 | tf_op jit(solution)/shard_map/ppermute | solution.py:38
  254.1 2.7 collective-permute-start.27
  259.5 4.1 %collective-permute-start.28 = (f32[16]{0:T(128)S(1)}, f32[16]{0:T(128)S(1)}, u32[]{:S(2)}, u32[]{:S(2)}) collective-permute-start(f32[16]{0:T(128)S(1)} %add.252), channel_id=1, source_target_pairs={{0,64},{32,96},{64,0},{96,32},{128,192},{160,224},{192,128},{224,1... | collective-permute-start | bytes 200 | tf_op jit(solution)/shard_map/ppermute | solution.py:38
  263.6 2.8 collective-permute-done.28
  266.4 2.7 collective-permute-start.29
  269.2 2.7 collective-permute-done.29
  271.8 4.0 %collective-permute-start.30 = (f32[16]{0:T(128)S(1)}, f32[16]{0:T(128)S(1)}, u32[]{:S(2)}, u32[]{:S(2)}) collective-permute-start(f32[16]{0:T(128)S(1)} %add.254), channel_id=1, source_target_pairs={{0,256},{32,288},{64,320},{96,352},{128,384},{160,416},{192,448},{... | collective-permute-start | bytes 200 | tf_op jit(solution)/shard_map/ppermute | solution.py:38
  275.8 2.9 collective-permute-done.30
  281.4 2.3 gather_fusion.5
  283.8 3.6 convolution_bitcast_fusion.4
  290.2 34.7 %fusion.26 = f32[16,16,256]{2,0,1:T(8,128)S(1)} fusion(f32[16,16,5,256]{3,0,2,1:T(8,128)} %bitcast.128, f32[16,5]{1,0:T(8,128)S(1)} %copy-done.40, f32[16,5,256]{2,1,0:T(8,128)} %get-tuple-element.18, f32[16,256]{1,0:T(8,128)S(1)} %copy-done.33, f32[16,5,256]{2,1,0:T(8,128)} %get-tuple-element.17, f32[16,256]{1,0:T(8,128)S(1)} %copy-done.35, ...), kind=kOutput, calls=%fused_computation.36 | convolution fusion | flops 1080164352 | bytes 2146624 | tf_op jit(solution)/shard_map/lspq,mlsq->mlp/dot_general | solution.py:108
  326.7 2.4 collective-permute-start.33
  329.9 2.2 collective-permute-start.34
  332.1 3.2 collective-permute-done.34
  335.3 4.7 %collective-permute-start.35 = (f32[16]{0:T(128)S(1)}, f32[16]{0:T(128)S(1)}, u32[]{:S(2)}, u32[]{:S(2)}) collective-permute-start(f32[16]{0:T(128)S(1)} %add.263), channel_id=1, source_target_pairs={{0,4},{1,5},{2,6},{3,7},{4,0},{5,1},{6,2},{7,3},{8,12},{9,13},{10,... | collective-permute-start | bytes 200 | tf_op jit(solution)/shard_map/ppermute | solution.py:38
  341.6 4.4 %collective-permute-start.36 = (f32[16]{0:T(128)S(1)}, f32[16]{0:T(128)S(1)}, u32[]{:S(2)}, u32[]{:S(2)}) collective-permute-start(f32[16]{0:T(128)S(1)} %add.264), channel_id=1, source_target_pairs={{0,8},{1,9},{2,10},{3,11},{4,12},{5,13},{6,14},{7,15},{8,0},{9,1},... | collective-permute-start | bytes 200 | tf_op jit(solution)/shard_map/ppermute | solution.py:38
  346.0 4.9 %collective-permute-done.36 = f32[16]{0:T(128)S(1)} collective-permute-done((f32[16]{0:T(128)S(1)}, f32[16]{0:T(128)S(1)}, u32[]{:S(2)}, u32[]{:S(2)}) %collective-permute-start.36) | collective-permute-done | bytes 96 | tf_op jit(solution)/shard_map/ppermute | solution.py:38
  350.9 5.5 %collective-permute-start.37 = (f32[16]{0:T(128)S(1)}, f32[16]{0:T(128)S(1)}, u32[]{:S(2)}, u32[]{:S(2)}) collective-permute-start(f32[16]{0:T(128)S(1)} %add.265), channel_id=1, source_target_pairs={{0,16},{1,17},{2,18},{3,19},{4,20},{5,21},{6,22},{7,23},{8,24},{9,... | collective-permute-start | bytes 200 | tf_op jit(solution)/shard_map/ppermute | solution.py:38
  356.4 8.7 %collective-permute-done.37 = f32[16]{0:T(128)S(1)} collective-permute-done((f32[16]{0:T(128)S(1)}, f32[16]{0:T(128)S(1)}, u32[]{:S(2)}, u32[]{:S(2)}) %collective-permute-start.37) | collective-permute-done | bytes 96 | tf_op jit(solution)/shard_map/ppermute | solution.py:38
  365.1 2.6 collective-permute-start.38
  367.7 2.8 collective-permute-done.38
  370.5 3.9 %collective-permute-start.39 = (f32[16]{0:T(128)S(1)}, f32[16]{0:T(128)S(1)}, u32[]{:S(2)}, u32[]{:S(2)}) collective-permute-start(f32[16]{0:T(128)S(1)} %add.267), channel_id=1, source_target_pairs={{0,64},{32,96},{64,0},{96,32},{128,192},{160,224},{192,128},{224,1... | collective-permute-start | bytes 200 | tf_op jit(solution)/shard_map/ppermute | solution.py:38
  374.5 3.0 collective-permute-done.39
  377.4 2.7 collective-permute-start.40
  380.2 2.7 collective-permute-done.40
  382.9 3.8 collective-permute-start.41
  386.7 3.1 collective-permute-done.41
  (204 shorter events, 50.1 us)
Async XLA Ops:
  0.6 89.4 %copy-start = (f32[16,4,64,64]{3,2,1,0:T(8,128)S(1)}, f32[16,4,64,64]{3,2,1,0:T(8,128)}, u32[]{:S(2)}) copy-start(f32[16,4,64,64]{3,2,1,0:T(8,128)} %param.15) | copy-start | bytes 3145732
  0.6 19.0 %copy-start.23 = (f32[3,16,256]{2,1,0:T(8,128)S(1)}, f32[3,16,256]{2,1,0:T(8,128)}, u32[]{:S(2)}) copy-start(f32[3,16,256]{2,1,0:T(8,128)} %param.13) | copy-start | bytes 147460
  0.7 16.8 %copy-start.29 = (s32[16,5]{0,1:T(8,128)S(1)}, s32[16,5]{0,1:T(8,128)}, u32[]{:S(2)}) copy-start(s32[16,5]{0,1:T(8,128)} %param.18) | copy-start | bytes 964
  0.7 17.4 %copy-start.42 = (s32[2,2]{1,0:T(2,128)S(1)}, s32[2,2]{1,0:T(2,128)}, u32[]{:S(2)}) copy-start(s32[2,2]{1,0:T(2,128)} %param.20) | copy-start | bytes 52
  0.7 17.5 %copy-start.41 = (s32[16,4]{0,1:T(4,128)S(1)}, s32[16,4]{0,1:T(4,128)}, u32[]{:S(2)}) copy-start(s32[16,4]{0,1:T(4,128)} %param.19) | copy-start | bytes 772
  0.7 19.5 %copy-start.6 = (f32[16,64,64]{2,1,0:T(8,128)S(1)}, f32[16,64,64]{2,1,0:T(8,128)}, u32[]{:S(2)}) copy-start(f32[16,64,64]{2,1,0:T(8,128)} %param.16) | copy-start | bytes 786436
  0.7 20.1 %copy-start.37 = (s32[16]{0:T(128)S(1)}, s32[16]{0:T(128)}, u32[]{:S(2)}) copy-start(s32[16]{0:T(128)} %param.21) | copy-start | bytes 196
  2.5 41.7 %collective-permute-start = (f32[16]{0:T(128)}, f32[16]{0:T(128)}, u32[]{:S(2)}, u32[]{:S(2)}) collective-permute-start(f32[16]{0:T(128)} %multiply_reduce_fusion.3), channel_id=1, source_target_pairs={{0,1},{1,0},{2,3},{3,2},{4,5},{5,4},{6,7},{7,6},{8,9},{9,8},{10,11... | collective-permute-start | bytes 200 | tf_op jit(solution)/shard_map/ppermute | solution.py:38
  5.3 37.0 %copy-start.19 = (f32[2,2,64,64]{3,2,1,0:T(8,128)S(1)}, f32[2,2,64,64]{3,2,1,0:T(8,128)}, u32[]{:S(2)}) copy-start(f32[2,2,64,64]{3,2,1,0:T(8,128)} %param.17) | copy-start | bytes 196612
  5.9 76.4 %collective-permute-start.11 = (f32[3,2,256]{2,0,1:T(4,128)}, f32[3,2,256]{2,0,1:T(4,128)}, u32[]{:S(2)}, u32[]{:S(2)}) collective-permute-start(f32[3,2,256]{2,0,1:T(4,128)} %get-tuple-element.23), channel_id=1, source_target_pairs={{0,1},{1,2},{2,3},{3,4},{4,5},{5,6},{6,7},{7,8},{8,9},{9,10},{10,1... | collective-permute-start | bytes 18440 | tf_op jit(solution)/shard_map/ppermute | solution.py:21
  6.4 75.9 %collective-permute-start.12 = (f32[3,2,256]{2,0,1:T(4,128)}, f32[3,2,256]{2,0,1:T(4,128)}, u32[]{:S(2)}, u32[]{:S(2)}) collective-permute-start(f32[3,2,256]{2,0,1:T(4,128)} %get-tuple-element.24), channel_id=1, source_target_pairs={{1,0},{2,1},{3,2},{4,3},{5,4},{6,5},{7,6},{8,7},{9,8},{10,9},{11,1... | collective-permute-start | bytes 18440 | tf_op jit(solution)/shard_map/ppermute | solution.py:23
  15.7 69.2 %collective-permute-start.9 = (f32[16,6,320]{2,0,1:T(8,128)}, f32[16,6,320]{2,0,1:T(8,128)}, u32[]{:S(2)}, u32[]{:S(2)}) collective-permute-start(f32[16,6,320]{2,0,1:T(8,128)} %get-tuple-element.19), channel_id=1, source_target_pairs={{0,1},{1,2},{2,3},{3,4},{4,5},{5,6},{6,7},{7,8},{8,9},{9,10},{10,1... | collective-permute-start | bytes 368648 | tf_op jit(solution)/shard_map/ppermute | solution.py:21
  15.7 69.2 %collective-permute-start.10 = (f32[16,6,320]{2,0,1:T(8,128)}, f32[16,6,320]{2,0,1:T(8,128)}, u32[]{:S(2)}, u32[]{:S(2)}) collective-permute-start(f32[16,6,320]{2,0,1:T(8,128)} %get-tuple-element.20), channel_id=1, source_target_pairs={{1,0},{2,1},{3,2},{4,3},{5,4},{6,5},{7,6},{8,7},{9,8},{10,9},{11,1... | collective-permute-start | bytes 368648 | tf_op jit(solution)/shard_map/ppermute | solution.py:23
  18.8 23.4 %copy-start.36 = (s32[1024]{0:T(1024)}, s32[1024]{0:T(1024)S(1)}, u32[]{:S(2)}) copy-start(s32[1024]{0:T(1024)S(1)} %pad_clamp_fusion) | copy-start | bytes 12292
  44.9 12.1 %collective-permute-start.1 = (f32[16]{0:T(128)S(1)}, f32[16]{0:T(128)S(1)}, u32[]{:S(2)}, u32[]{:S(2)}) collective-permute-start(f32[16]{0:T(128)S(1)} %add.208), channel_id=1, source_target_pairs={{0,2},{1,3},{2,0},{3,1},{4,6},{5,7},{6,4},{7,5},{8,10},{9,11},{10,... | collective-permute-start | bytes 200 | tf_op jit(solution)/shard_map/ppermute | solution.py:38
  57.0 6.3 %collective-permute-start.2 = (f32[16]{0:T(128)S(1)}, f32[16]{0:T(128)S(1)}, u32[]{:S(2)}, u32[]{:S(2)}) collective-permute-start(f32[16]{0:T(128)S(1)} %add.209), channel_id=1, source_target_pairs={{0,4},{1,5},{2,6},{3,7},{4,0},{5,1},{6,2},{7,3},{8,12},{9,13},{10,... | collective-permute-start | bytes 200 | tf_op jit(solution)/shard_map/ppermute | solution.py:38
  63.3 9.3 %collective-permute-start.3 = (f32[16]{0:T(128)S(1)}, f32[16]{0:T(128)S(1)}, u32[]{:S(2)}, u32[]{:S(2)}) collective-permute-start(f32[16]{0:T(128)S(1)} %add.210), channel_id=1, source_target_pairs={{0,8},{1,9},{2,10},{3,11},{4,12},{5,13},{6,14},{7,15},{8,0},{9,1},... | collective-permute-start | bytes 200 | tf_op jit(solution)/shard_map/ppermute | solution.py:38
  73.2 55.8 %collective-permute-start.4 = (f32[16]{0:T(128)}, f32[16]{0:T(128)}, u32[]{:S(2)}, u32[]{:S(2)}) collective-permute-start(f32[16]{0:T(128)} %add.211), channel_id=1, source_target_pairs={{0,16},{1,17},{2,18},{3,19},{4,20},{5,21},{6,22},{7,23},{8,24},{9,... | collective-permute-start | bytes 200 | tf_op jit(solution)/shard_map/ppermute | solution.py:38
  94.0 32.3 %copy-start.1 = (f32[16,256,64]{1,2,0:T(8,128)S(1)}, f32[16,256,64]{1,2,0:T(8,128)}, u32[]{:S(2)}) copy-start(f32[16,256,64]{1,2,0:T(8,128)} %param.14) | copy-start | bytes 3145732
  126.3 71.5 %copy-start.7 = (f32[16,64,64]{2,1,0:T(8,128)S(1)}, f32[16,64,64]{2,1,0:T(8,128)}, u32[]{:S(2)}) copy-start(f32[16,64,64]{2,1,0:T(8,128)} %param.16) | copy-start | bytes 786436
  126.3 72.1 %copy-start.38 = (s32[16]{0:T(128)S(1)}, s32[16]{0:T(128)}, u32[]{:S(2)}) copy-start(s32[16]{0:T(128)} %param.21) | copy-start | bytes 196
  127.1 71.3 %copy-start.9 = (f32[16,16,256]{2,0,1:T(8,128)}, f32[16,16,256]{2,0,1:T(8,128)S(1)}, u32[]{:S(2)}) copy-start(f32[16,16,256]{2,0,1:T(8,128)S(1)} %get-tuple-element.29) | copy-start | bytes 786436
  127.1 3.0 collective-permute-start.13
  130.1 7.0 %collective-permute-start.14 = (f32[16]{0:T(128)S(1)}, f32[16]{0:T(128)S(1)}, u32[]{:S(2)}, u32[]{:S(2)}) collective-permute-start(f32[16]{0:T(128)S(1)} %add.238), channel_id=1, source_target_pairs={{0,2},{1,3},{2,0},{3,1},{4,6},{5,7},{6,4},{7,5},{8,10},{9,11},{10,... | collective-permute-start | bytes 200 | tf_op jit(solution)/shard_map/ppermute | solution.py:38
  134.1 5.4 %collective-permute-start.5 = (f32[16]{0:T(128)S(1)}, f32[16]{0:T(128)S(1)}, u32[]{:S(2)}, u32[]{:S(2)}) collective-permute-start(f32[16]{0:T(128)S(1)} %add.212), channel_id=1, source_target_pairs={{0,32},{32,0},{64,96},{96,64},{128,160},{160,128},{192,224},{224,1... | collective-permute-start | bytes 200 | tf_op jit(solution)/shard_map/ppermute | solution.py:38
  137.2 6.3 %collective-permute-start.15 = (f32[16]{0:T(128)S(1)}, f32[16]{0:T(128)S(1)}, u32[]{:S(2)}, u32[]{:S(2)}) collective-permute-start(f32[16]{0:T(128)S(1)} %add.239), channel_id=1, source_target_pairs={{0,4},{1,5},{2,6},{3,7},{4,0},{5,1},{6,2},{7,3},{8,12},{9,13},{10,... | collective-permute-start | bytes 200 | tf_op jit(solution)/shard_map/ppermute | solution.py:38
  143.5 9.3 %collective-permute-start.16 = (f32[16]{0:T(128)S(1)}, f32[16]{0:T(128)S(1)}, u32[]{:S(2)}, u32[]{:S(2)}) collective-permute-start(f32[16]{0:T(128)S(1)} %add.240), channel_id=1, source_target_pairs={{0,8},{1,9},{2,10},{3,11},{4,12},{5,13},{6,14},{7,15},{8,0},{9,1},... | collective-permute-start | bytes 200 | tf_op jit(solution)/shard_map/ppermute | solution.py:38
  147.8 10.5 %collective-permute-start.6 = (f32[16]{0:T(128)S(1)}, f32[16]{0:T(128)S(1)}, u32[]{:S(2)}, u32[]{:S(2)}) collective-permute-start(f32[16]{0:T(128)S(1)} %add.213), channel_id=1, source_target_pairs={{0,64},{32,96},{64,0},{96,32},{128,192},{160,224},{192,128},{224,1... | collective-permute-start | bytes 200 | tf_op jit(solution)/shard_map/ppermute | solution.py:38
  152.9 14.1 %collective-permute-start.17 = (f32[16]{0:T(128)S(1)}, f32[16]{0:T(128)S(1)}, u32[]{:S(2)}, u32[]{:S(2)}) collective-permute-start(f32[16]{0:T(128)S(1)} %add.241), channel_id=1, source_target_pairs={{0,16},{1,17},{2,18},{3,19},{4,20},{5,21},{6,22},{7,23},{8,24},{9,... | collective-permute-start | bytes 200 | tf_op jit(solution)/shard_map/ppermute | solution.py:38
  167.0 5.8 %collective-permute-start.18 = (f32[16]{0:T(128)S(1)}, f32[16]{0:T(128)S(1)}, u32[]{:S(2)}, u32[]{:S(2)}) collective-permute-start(f32[16]{0:T(128)S(1)} %add.242), channel_id=1, source_target_pairs={{0,32},{32,0},{64,96},{96,64},{128,160},{160,128},{192,224},{224,1... | collective-permute-start | bytes 200 | tf_op jit(solution)/shard_map/ppermute | solution.py:38
  169.7 7.3 %collective-permute-start.7 = (f32[16]{0:T(128)S(1)}, f32[16]{0:T(128)S(1)}, u32[]{:S(2)}, u32[]{:S(2)}) collective-permute-start(f32[16]{0:T(128)S(1)} %add.214), channel_id=1, source_target_pairs={{0,128},{32,160},{64,192},{96,224},{128,0},{160,32},{192,64},{224,... | collective-permute-start | bytes 200 | tf_op jit(solution)/shard_map/ppermute | solution.py:38
  172.9 6.9 %collective-permute-start.19 = (f32[16]{0:T(128)S(1)}, f32[16]{0:T(128)S(1)}, u32[]{:S(2)}, u32[]{:S(2)}) collective-permute-start(f32[16]{0:T(128)S(1)} %add.243), channel_id=1, source_target_pairs={{0,64},{32,96},{64,0},{96,32},{128,192},{160,224},{192,128},{224,1... | collective-permute-start | bytes 200 | tf_op jit(solution)/shard_map/ppermute | solution.py:38
  179.8 7.3 %collective-permute-start.20 = (f32[16]{0:T(128)S(1)}, f32[16]{0:T(128)S(1)}, u32[]{:S(2)}, u32[]{:S(2)}) collective-permute-start(f32[16]{0:T(128)S(1)} %add.244), channel_id=1, source_target_pairs={{0,128},{32,160},{64,192},{96,224},{128,0},{160,32},{192,64},{224,... | collective-permute-start | bytes 200 | tf_op jit(solution)/shard_map/ppermute | solution.py:38
  182.6 7.4 %collective-permute-start.8 = (f32[16]{0:T(128)S(1)}, f32[16]{0:T(128)S(1)}, u32[]{:S(2)}, u32[]{:S(2)}) collective-permute-start(f32[16]{0:T(128)S(1)} %add.215), channel_id=1, source_target_pairs={{0,256},{32,288},{64,320},{96,352},{128,384},{160,416},{192,448},{... | collective-permute-start | bytes 200 | tf_op jit(solution)/shard_map/ppermute | solution.py:38
  187.2 6.9 %collective-permute-start.21 = (f32[16]{0:T(128)S(1)}, f32[16]{0:T(128)S(1)}, u32[]{:S(2)}, u32[]{:S(2)}) collective-permute-start(f32[16]{0:T(128)S(1)} %add.245), channel_id=1, source_target_pairs={{0,256},{32,288},{64,320},{96,352},{128,384},{160,416},{192,448},{... | collective-permute-start | bytes 200 | tf_op jit(solution)/shard_map/ppermute | solution.py:38
  194.9 88.8 %copy-start.4 = (f32[16,16,256]{2,0,1:T(8,128)}, f32[16,16,256]{2,0,1:T(8,128)S(1)}, u32[]{:S(2)}) copy-start(f32[16,16,256]{2,0,1:T(8,128)S(1)} %get-tuple-element.11) | copy-start | bytes 786436
  194.9 3.7 collective-permute-start.22
  196.8 84.6 %copy-start.28 = (s32[1024]{0:T(1024)S(1)}, s32[1024]{0:T(1024)}, u32[]{:S(2)}) copy-start(s32[1024]{0:T(1024)} %pad_clamp_fusion.1) | copy-start | bytes 12292
  197.8 85.9 %copy-start.12 = (f32[16,16,64]{2,0,1:T(8,128)}, f32[16,16,64]{2,0,1:T(8,128)S(1)}, u32[]{:S(2)}) copy-start(f32[16,16,64]{2,0,1:T(8,128)S(1)} %convolution_bitcast_fusion.8) | copy-start | bytes 196612
  198.6 5.4 %collective-permute-start.23 = (f32[16]{0:T(128)S(1)}, f32[16]{0:T(128)S(1)}, u32[]{:S(2)}, u32[]{:S(2)}) collective-permute-start(f32[16]{0:T(128)S(1)} %add.247), channel_id=1, source_target_pairs={{0,2},{1,3},{2,0},{3,1},{4,6},{5,7},{6,4},{7,5},{8,10},{9,11},{10,... | collective-permute-start | bytes 200 | tf_op jit(solution)/shard_map/ppermute | solution.py:38
  204.0 25.9 %collective-permute-start.24 = (f32[16]{0:T(128)S(1)}, f32[16]{0:T(128)S(1)}, u32[]{:S(2)}, u32[]{:S(2)}) collective-permute-start(f32[16]{0:T(128)S(1)} %add.248), channel_id=1, source_target_pairs={{0,4},{1,5},{2,6},{3,7},{4,0},{5,1},{6,2},{7,3},{8,12},{9,13},{10,... | collective-permute-start | bytes 200 | tf_op jit(solution)/shard_map/ppermute | solution.py:38
  229.9 9.3 %collective-permute-start.25 = (f32[16]{0:T(128)S(1)}, f32[16]{0:T(128)}, u32[]{:S(2)}, u32[]{:S(2)}) collective-permute-start(f32[16]{0:T(128)S(1)} %add.249), channel_id=1, source_target_pairs={{0,8},{1,9},{2,10},{3,11},{4,12},{5,13},{6,14},{7,15},{8,0},{9,1},... | collective-permute-start | bytes 200 | tf_op jit(solution)/shard_map/ppermute | solution.py:38
  239.9 14.1 %collective-permute-start.26 = (f32[16]{0:T(128)S(1)}, f32[16]{0:T(128)S(1)}, u32[]{:S(2)}, u32[]{:S(2)}) collective-permute-start(f32[16]{0:T(128)S(1)} %add.250), channel_id=1, source_target_pairs={{0,16},{1,17},{2,18},{3,19},{4,20},{5,21},{6,22},{7,23},{8,24},{9,... | collective-permute-start | bytes 200 | tf_op jit(solution)/shard_map/ppermute | solution.py:38
  254.1 5.4 %collective-permute-start.27 = (f32[16]{0:T(128)S(1)}, f32[16]{0:T(128)S(1)}, u32[]{:S(2)}, u32[]{:S(2)}) collective-permute-start(f32[16]{0:T(128)S(1)} %add.251), channel_id=1, source_target_pairs={{0,32},{32,0},{64,96},{96,64},{128,160},{160,128},{192,224},{224,1... | collective-permute-start | bytes 200 | tf_op jit(solution)/shard_map/ppermute | solution.py:38
  259.5 6.9 %collective-permute-start.28 = (f32[16]{0:T(128)S(1)}, f32[16]{0:T(128)S(1)}, u32[]{:S(2)}, u32[]{:S(2)}) collective-permute-start(f32[16]{0:T(128)S(1)} %add.252), channel_id=1, source_target_pairs={{0,64},{32,96},{64,0},{96,32},{128,192},{160,224},{192,128},{224,1... | collective-permute-start | bytes 200 | tf_op jit(solution)/shard_map/ppermute | solution.py:38
  266.4 5.4 %collective-permute-start.29 = (f32[16]{0:T(128)S(1)}, f32[16]{0:T(128)S(1)}, u32[]{:S(2)}, u32[]{:S(2)}) collective-permute-start(f32[16]{0:T(128)S(1)} %add.253), channel_id=1, source_target_pairs={{0,128},{32,160},{64,192},{96,224},{128,0},{160,32},{192,64},{224,... | collective-permute-start | bytes 200 | tf_op jit(solution)/shard_map/ppermute | solution.py:38
  269.1 10.2 %collective-permute-start.31 = (f32[16,6,320]{2,0,1:T(8,128)S(1)}, f32[16,6,320]{2,0,1:T(8,128)S(1)}, u32[]{:S(2)}, u32[]{:S(2)}) collective-permute-start(f32[16,6,320]{2,0,1:T(8,128)S(1)} %get-tuple-element.14), channel_id=1, source_target_pairs={{0,1},{1,2},{2,3},{3,4},{4,5},{5,6},{6,7},{7,8},{8,9},{9,10},{10,1... | collective-permute-start | bytes 368648 | tf_op jit(solution)/shard_map/ppermute | solution.py:21
  271.8 6.9 %collective-permute-start.30 = (f32[16]{0:T(128)S(1)}, f32[16]{0:T(128)S(1)}, u32[]{:S(2)}, u32[]{:S(2)}) collective-permute-start(f32[16]{0:T(128)S(1)} %add.254), channel_id=1, source_target_pairs={{0,256},{32,288},{64,320},{96,352},{128,384},{160,416},{192,448},{... | collective-permute-start | bytes 200 | tf_op jit(solution)/shard_map/ppermute | solution.py:38
  275.8 3.6 collective-permute-start.32
  290.1 34.7 %copy-start.8 = (f32[16,64,64]{2,1,0:T(8,128)S(1)}, f32[16,64,64]{2,1,0:T(8,128)}, u32[]{:S(2)}) copy-start(f32[16,64,64]{2,1,0:T(8,128)} %param.16) | copy-start | bytes 786436
  290.2 34.7 %copy-start.18 = (f32[16,16,64]{2,1,0:T(8,128)S(1)}, f32[16,16,64]{2,1,0:T(8,128)}, u32[]{:S(2)}) copy-start(f32[16,16,64]{2,1,0:T(8,128)} %convolution_bitcast_fusion.2) | copy-start | bytes 196612
  290.2 34.7 %copy-start.20 = (f32[16,16,64]{2,1,0:T(8,128)S(1)}, f32[16,16,64]{2,1,0:T(8,128)}, u32[]{:S(2)}) copy-start(f32[16,16,64]{2,1,0:T(8,128)} %convolution_bitcast_fusion.4) | copy-start | bytes 196612
  290.2 35.6 %copy-start.3 = (f32[16,16,256]{2,1,0:T(8,128)S(1)}, f32[16,16,256]{2,1,0:T(8,128)}, u32[]{:S(2)}) copy-start(f32[16,16,256]{2,1,0:T(8,128)} %param.11) | copy-start | bytes 786436
  290.2 35.6 %copy-start.5 = (f32[16,16,256]{2,0,1:T(8,128)S(1)}, f32[16,16,256]{2,0,1:T(8,128)}, u32[]{:S(2)}) copy-start(f32[16,16,256]{2,0,1:T(8,128)} %copy-done.4) | copy-start | bytes 786436
  290.2 35.6 %copy-start.10 = (f32[16,16,256]{2,0,1:T(8,128)S(1)}, f32[16,16,256]{2,0,1:T(8,128)}, u32[]{:S(2)}) copy-start(f32[16,16,256]{2,0,1:T(8,128)} %copy-done.9) | copy-start | bytes 786436
  326.7 3.2 collective-permute-start.33
  329.9 5.4 %collective-permute-start.34 = (f32[16]{0:T(128)S(1)}, f32[16]{0:T(128)S(1)}, u32[]{:S(2)}, u32[]{:S(2)}) collective-permute-start(f32[16]{0:T(128)S(1)} %add.262), channel_id=1, source_target_pairs={{0,2},{1,3},{2,0},{3,1},{4,6},{5,7},{6,4},{7,5},{8,10},{9,11},{10,... | collective-permute-start | bytes 200 | tf_op jit(solution)/shard_map/ppermute | solution.py:38
  335.3 6.3 %collective-permute-start.35 = (f32[16]{0:T(128)S(1)}, f32[16]{0:T(128)S(1)}, u32[]{:S(2)}, u32[]{:S(2)}) collective-permute-start(f32[16]{0:T(128)S(1)} %add.263), channel_id=1, source_target_pairs={{0,4},{1,5},{2,6},{3,7},{4,0},{5,1},{6,2},{7,3},{8,12},{9,13},{10,... | collective-permute-start | bytes 200 | tf_op jit(solution)/shard_map/ppermute | solution.py:38
  341.6 9.3 %collective-permute-start.36 = (f32[16]{0:T(128)S(1)}, f32[16]{0:T(128)S(1)}, u32[]{:S(2)}, u32[]{:S(2)}) collective-permute-start(f32[16]{0:T(128)S(1)} %add.264), channel_id=1, source_target_pairs={{0,8},{1,9},{2,10},{3,11},{4,12},{5,13},{6,14},{7,15},{8,0},{9,1},... | collective-permute-start | bytes 200 | tf_op jit(solution)/shard_map/ppermute | solution.py:38
  350.9 14.1 %collective-permute-start.37 = (f32[16]{0:T(128)S(1)}, f32[16]{0:T(128)S(1)}, u32[]{:S(2)}, u32[]{:S(2)}) collective-permute-start(f32[16]{0:T(128)S(1)} %add.265), channel_id=1, source_target_pairs={{0,16},{1,17},{2,18},{3,19},{4,20},{5,21},{6,22},{7,23},{8,24},{9,... | collective-permute-start | bytes 200 | tf_op jit(solution)/shard_map/ppermute | solution.py:38
  365.1 5.4 %collective-permute-start.38 = (f32[16]{0:T(128)S(1)}, f32[16]{0:T(128)S(1)}, u32[]{:S(2)}, u32[]{:S(2)}) collective-permute-start(f32[16]{0:T(128)S(1)} %add.266), channel_id=1, source_target_pairs={{0,32},{32,0},{64,96},{96,64},{128,160},{160,128},{192,224},{224,1... | collective-permute-start | bytes 200 | tf_op jit(solution)/shard_map/ppermute | solution.py:38
  370.5 6.9 %collective-permute-start.39 = (f32[16]{0:T(128)S(1)}, f32[16]{0:T(128)S(1)}, u32[]{:S(2)}, u32[]{:S(2)}) collective-permute-start(f32[16]{0:T(128)S(1)} %add.267), channel_id=1, source_target_pairs={{0,64},{32,96},{64,0},{96,32},{128,192},{160,224},{192,128},{224,1... | collective-permute-start | bytes 200 | tf_op jit(solution)/shard_map/ppermute | solution.py:38
  377.4 5.4 %collective-permute-start.40 = (f32[16]{0:T(128)S(1)}, f32[16]{0:T(128)S(1)}, u32[]{:S(2)}, u32[]{:S(2)}) collective-permute-start(f32[16]{0:T(128)S(1)} %add.268), channel_id=1, source_target_pairs={{0,128},{32,160},{64,192},{96,224},{128,0},{160,32},{192,64},{224,... | collective-permute-start | bytes 200 | tf_op jit(solution)/shard_map/ppermute | solution.py:38
  382.9 6.9 %collective-permute-start.41 = (f32[16]{0:T(128)S(1)}, f32[16]{0:T(128)S(1)}, u32[]{:S(2)}, u32[]{:S(2)}) collective-permute-start(f32[16]{0:T(128)S(1)} %add.269), channel_id=1, source_target_pairs={{0,256},{32,288},{64,320},{96,352},{128,384},{160,416},{192,448},{... | collective-permute-start | bytes 200 | tf_op jit(solution)/shard_map/ppermute | solution.py:38
  (22 other events, 67.7 us)
where the time goes:
time: 394 us; the launch traced here: 392 us
  starting transfers between devices  140 us (36%)
  waiting for transfers between devices  85.8 us (22%)
  matrix products  85 us (22%)
  blocking collectives  44.7 us (11%)
  local copies, waits for them, and re-layouts  20.7 us (5%)
  other arithmetic  13.6 us (3%)
    ppermute x36, starting transfers between devices, all_sum(): lax.ppermute(vector, axis, [(i, i ^ stride) for i in range(count)])  133 us
    ppermute x36, waiting for transfers between devices, all_sum(): lax.ppermute(vector, axis, [(i, i ^ stride) for i in range(count)])  85.8 us
    dot_general x2, matrix products, covariance_apply(): jnp.einsum('lspq,mlsq->mlp', near_blocks, rim_values[:, near_rows], preci...  66.9 us
    all_gather x2, blocking collectives, covariance_apply(): band_coeffs = lax.all_gather(panel_coeffs, 'band', axis=1, tiled=True)  44.7 us
  transfers between devices with their start and end apart: 42, of which 26 were waited for; matrix products, arithmetic and copies ran while one was open for 17% of the time, Pallas kernels for 0%

commit v1 on v0

--- a/solution.py
+++ b/solution.py
@@ -113,7 +113,15 @@
         )
         upward = jnp.einsum("lab,mla->mlb", transfer, coeffs, precision=HIGHEST_PRECISION)
         panel_coeffs = jnp.einsum("lk,mlb->mkb", membership, upward, precision=HIGHEST_PRECISION)
-        band_coeffs = lax.all_gather(panel_coeffs, "band", axis=1, tiled=True)
+        band_coeffs = jnp.concatenate(
+            lax.all_to_all(
+                jnp.stack(lax.axis_size("band") * [panel_coeffs], 0),
+                axis_name="band",
+                split_axis=0,
+                concat_axis=0,
+            ),
+            1,
+        )
         panel_far = jnp.einsum(
             "ksab,mksb->mka",
             panel_couple,

time: 394 us -> 376 us (0.954)
  the two profiles are of different devices: /device:TPU:32 before, /device:TPU:2 now
where the time goes in v1:
time: 376 us; the launch traced here: 374 us
  starting transfers between devices  149 us (40%)
  waiting for transfers between devices  91 us (24%)
  matrix products  86.2 us (23%)
  local copies, waits for them, and re-layouts  25.8 us (7%)
  other arithmetic  20.1 us (5%)
    ppermute x36, starting transfers between devices, all_sum(): lax.ppermute(vector, axis, [(i, i ^ stride) for i in range(count)])  123 us
    ppermute x36, waiting for transfers between devices, all_sum(): lax.ppermute(vector, axis, [(i, i ^ stride) for i in range(count)])  91 us
    dot_general x2, matrix products, covariance_apply(): jnp.einsum('lspq,mlsq->mlp', near_blocks, rim_values[:, near_rows], preci...  66.7 us
    all_to_all x2, starting transfers between devices, covariance_apply(): lax.all_to_all(jnp.stack(lax.axis_size('band') * [panel_coeffs], 0), axis...  12.9 us
    ppermute x3, starting transfers between devices, extended(): lax.ppermute(head, axis, [((i + 1) % count, i) for i in range(count)])  12.1 us
    unnamed x96, local copies, waits for them, and re-layouts  8.14 us
  transfers between devices with their start and end apart: 44, of which 26 were waited for; matrix products, arithmetic and copies ran while one was open for 20% of the time, Pallas kernels for 0%

profile of v1, /device:TPU:2, one launch (start us, length us, event | category | flops | bytes accessed | tf_op | source)
XLA Modules:
  0.0 373.7 jit_solution(9890674670201344755)
XLA Ops:
  2.5 1.9 collective-permute-start
  6.3 9.1 %collective-permute-start.12 = (f32[3,2,256]{2,0,1:T(4,128)}, f32[3,2,256]{2,0,1:T(4,128)S(1)}, u32[]{:S(2)}, u32[]{:S(2)}) collective-permute-start(f32[3,2,256]{2,0,1:T(4,128)} %get-tuple-element.22), channel_id=1, source_target_pairs={{1,0},{2,1},{3,2},{4,3},{5,4},{6,5},{7,6},{8,7},{9,8},{10,9},{11,1... | collective-permute-start | bytes 18440 | tf_op jit(solution)/shard_map/ppermute | solution.py:23
  15.5 2.4 convolution_bitcast_fusion.7
  19.5 7.5 %all-to-all-start = ((f32[16,1,2048]{2,1,0:T(1,128)}), f32[16,1,2048]{2,1,0:T(1,128)}, u32[]{:S(2)}, u32[]{:S(2)}) async-start(f32[16,1,2048]{2,1,0:T(1,128)} %reshape.113), calls=%async_computation | async-start | bytes 262144 | tf_op jit(solution)/shard_map/all_to_all | solution.py:117
  27.9 3.0 collective-permute-start.10
  35.8 3.4 collective-permute-done.1
  41.7 3.8 %collective-permute-done.2 = f32[16]{0:T(128)S(1)} collective-permute-done((f32[16]{0:T(128)S(1)}, f32[16]{0:T(128)S(1)}, u32[]{:S(2)}, u32[]{:S(2)}) %collective-permute-start.2) | collective-permute-done | bytes 96 | tf_op jit(solution)/shard_map/ppermute | solution.py:38
  45.5 2.4 collective-permute-start.3
  48.6 6.2 %collective-permute-done.3 = f32[16]{0:T(128)S(1)} collective-permute-done((f32[16]{0:T(128)S(1)}, f32[16]{0:T(128)S(1)}, u32[]{:S(2)}, u32[]{:S(2)}) %collective-permute-start.3) | collective-permute-done | bytes 96 | tf_op jit(solution)/shard_map/ppermute | solution.py:38
  55.5 9.1 %collective-permute-start.4 = (f32[16]{0:T(128)}, f32[16]{0:T(128)}, u32[]{:S(2)}, u32[]{:S(2)}) collective-permute-start(f32[16]{0:T(128)} %add.211), channel_id=1, source_target_pairs={{0,16},{1,17},{2,18},{3,19},{4,20},{5,21},{6,22},{7,23},{8,24},{9,... | collective-permute-start | bytes 200 | tf_op jit(solution)/shard_map/ppermute | solution.py:38
  76.9 3.0 convolution_bitcast_fusion.5
  80.9 32.3 %fusion.27 = f32[16,16,256]{2,0,1:T(8,128)S(1)} fusion(f32[16,16,5,256]{3,0,2,1:T(8,128)S(1)} %bitcast.143, f32[16,5]{1,0:T(8,128)S(1)} %copy-done.34, f32[16,5,256]{2,1,0:T(8,128)S(1)} %copy-done.22, f32[16,256]{1,0:T(8,128)S(1)} %copy-done.28, f32[16,5,256]{2,1,0:T(8,128)S(1)} %copy-done.21, f32[16,256]{1,0:T(8,128)S(1)} %copy-done.30, ...), kind=kOutput, calls=%fused_computation.39 | convolution fusion | flops 1080164352 | bytes 2146624 | tf_op jit(solution)/shard_map/lspq,mlsq->mlp/dot_general | solution.py:108
  114.0 1.9 collective-permute-start.13
  117.1 1.9 collective-permute-start.14
  119.0 3.4 collective-permute-start.5
  124.4 4.4 %collective-permute-done.15 = f32[16]{0:T(128)S(1)} collective-permute-done((f32[16]{0:T(128)S(1)}, f32[16]{0:T(128)S(1)}, u32[]{:S(2)}, u32[]{:S(2)}) %collective-permute-start.15) | collective-permute-done | bytes 96 | tf_op jit(solution)/shard_map/ppermute | solution.py:38
  128.8 4.3 %collective-permute-start.16 = (f32[16]{0:T(128)S(1)}, f32[16]{0:T(128)S(1)}, u32[]{:S(2)}, u32[]{:S(2)}) collective-permute-start(f32[16]{0:T(128)S(1)} %add.240), channel_id=1, source_target_pairs={{0,8},{1,9},{2,10},{3,11},{4,12},{5,13},{6,14},{7,15},{8,0},{9,1},... | collective-permute-start | bytes 200 | tf_op jit(solution)/shard_map/ppermute | solution.py:38
  133.1 4.9 %collective-permute-start.6 = (f32[16]{0:T(128)S(1)}, f32[16]{0:T(128)S(1)}, u32[]{:S(2)}, u32[]{:S(2)}) collective-permute-start(f32[16]{0:T(128)S(1)} %add.213), channel_id=1, source_target_pairs={{0,64},{32,96},{64,0},{96,32},{128,192},{160,224},{192,128},{224,1... | collective-permute-start | bytes 200 | tf_op jit(solution)/shard_map/ppermute | solution.py:38
  138.1 5.5 %collective-permute-start.17 = (f32[16]{0:T(128)S(1)}, f32[16]{0:T(128)S(1)}, u32[]{:S(2)}, u32[]{:S(2)}) collective-permute-start(f32[16]{0:T(128)S(1)} %add.241), channel_id=1, source_target_pairs={{0,16},{1,17},{2,18},{3,19},{4,20},{5,21},{6,22},{7,23},{8,24},{9,... | collective-permute-start | bytes 200 | tf_op jit(solution)/shard_map/ppermute | solution.py:38
  143.7 8.6 %collective-permute-done.17 = f32[16]{0:T(128)S(1)} collective-permute-done((f32[16]{0:T(128)S(1)}, f32[16]{0:T(128)S(1)}, u32[]{:S(2)}, u32[]{:S(2)}) %collective-permute-start.17) | collective-permute-done | bytes 96 | tf_op jit(solution)/shard_map/ppermute | solution.py:38
  152.3 3.4 collective-permute-start.18
  155.7 2.5 collective-permute-start.7
  158.2 4.6 %collective-permute-start.19 = (f32[16]{0:T(128)S(1)}, f32[16]{0:T(128)S(1)}, u32[]{:S(2)}, u32[]{:S(2)}) collective-permute-start(f32[16]{0:T(128)S(1)} %add.243), channel_id=1, source_target_pairs={{0,64},{32,96},{64,0},{96,32},{128,192},{160,224},{192,128},{224,1... | collective-permute-start | bytes 200 | tf_op jit(solution)/shard_map/ppermute | solution.py:38
  162.8 2.3 collective-permute-done.19
  165.1 3.4 collective-permute-start.20
  168.5 4.0 %collective-permute-start.8 = (f32[16]{0:T(128)S(1)}, f32[16]{0:T(128)S(1)}, u32[]{:S(2)}, u32[]{:S(2)}) collective-permute-start(f32[16]{0:T(128)S(1)} %add.215), channel_id=1, source_target_pairs={{0,256},{32,288},{64,320},{96,352},{128,384},{160,416},{192,448},{... | collective-permute-start | bytes 200 | tf_op jit(solution)/shard_map/ppermute | solution.py:38
  172.5 3.4 collective-permute-start.21
  175.9 3.6 collective-permute-done.21
  180.2 2.1 collective-permute-start.22
  183.9 2.9 collective-permute-start.23
  187.0 2.3 collective-permute-done.23
  191.2 4.4 %collective-permute-done.24 = f32[16]{0:T(128)S(1)} collective-permute-done((f32[16]{0:T(128)S(1)}, f32[16]{0:T(128)S(1)}, u32[]{:S(2)}, u32[]{:S(2)}) %collective-permute-start.24) | collective-permute-done | bytes 96 | tf_op jit(solution)/shard_map/ppermute | solution.py:38
  195.6 4.4 %collective-permute-start.25 = (f32[16]{0:T(128)S(1)}, f32[16]{0:T(128)S(1)}, u32[]{:S(2)}, u32[]{:S(2)}) collective-permute-start(f32[16]{0:T(128)S(1)} %add.249), channel_id=1, source_target_pairs={{0,8},{1,9},{2,10},{3,11},{4,12},{5,13},{6,14},{7,15},{8,0},{9,1},... | collective-permute-start | bytes 200 | tf_op jit(solution)/shard_map/ppermute | solution.py:38
  200.8 4.2 %collective-permute-done.25 = f32[16]{0:T(128)S(1)} collective-permute-done((f32[16]{0:T(128)S(1)}, f32[16]{0:T(128)S(1)}, u32[]{:S(2)}, u32[]{:S(2)}) %collective-permute-start.25) | collective-permute-done | bytes 96 | tf_op jit(solution)/shard_map/ppermute | solution.py:38
  205.0 5.5 %collective-permute-start.26 = (f32[16]{0:T(128)S(1)}, f32[16]{0:T(128)S(1)}, u32[]{:S(2)}, u32[]{:S(2)}) collective-permute-start(f32[16]{0:T(128)S(1)} %add.250), channel_id=1, source_target_pairs={{0,16},{1,17},{2,18},{3,19},{4,20},{5,21},{6,22},{7,23},{8,24},{9,... | collective-permute-start | bytes 200 | tf_op jit(solution)/shard_map/ppermute | solution.py:38
  211.2 7.9 %collective-permute-done.26 = f32[16]{0:T(128)S(1)} collective-permute-done((f32[16]{0:T(128)S(1)}, f32[16]{0:T(128)S(1)}, u32[]{:S(2)}, u32[]{:S(2)}) %collective-permute-start.26) | collective-permute-done | bytes 96 | tf_op jit(solution)/shard_map/ppermute | solution.py:38
  219.6 2.5 collective-permute-start.27
  226.5 4.6 %collective-permute-start.28 = (f32[16]{0:T(128)}, f32[16]{0:T(128)}, u32[]{:S(2)}, u32[]{:S(2)}) collective-permute-start(f32[16]{0:T(128)} %add.252), channel_id=1, source_target_pairs={{0,64},{32,96},{64,0},{96,32},{128,192},{160,224},{192,128},{224,1... | collective-permute-start | bytes 200 | tf_op jit(solution)/shard_map/ppermute | solution.py:38
  231.1 5.4 %all-to-all-start.1 = ((f32[16,1,2048]{2,1,0:T(1,128)}), f32[16,1,2048]{2,1,0:T(1,128)}, u32[]{:S(2)}, u32[]{:S(2)}) async-start(f32[16,1,2048]{2,1,0:T(1,128)} %reshape.115), calls=%async_computation.1 | async-start | bytes 262144 | tf_op jit(solution)/shard_map/all_to_all | solution.py:117
  237.1 2.2 collective-permute-start.29
  239.3 3.2 collective-permute-done.29
  242.5 4.0 %collective-permute-start.30 = (f32[16]{0:T(128)S(1)}, f32[16]{0:T(128)S(1)}, u32[]{:S(2)}, u32[]{:S(2)}) collective-permute-start(f32[16]{0:T(128)S(1)} %add.254), channel_id=1, source_target_pairs={{0,256},{32,288},{64,320},{96,352},{128,384},{160,416},{192,448},{... | collective-permute-start | bytes 200 | tf_op jit(solution)/shard_map/ppermute | solution.py:38
  246.6 2.9 collective-permute-done.30
  250.5 2.5 reduce.1
  254.8 2.2 gather_fusion.6
  260.3 2.4 gather_fusion.5
  262.7 3.5 convolution_bitcast_fusion.4
  272.4 34.5 %fusion.26 = f32[16,16,256]{2,0,1:T(8,128)S(1)} fusion(f32[16,16,5,256]{3,0,2,1:T(8,128)} %bitcast.144, f32[16,5]{1,0:T(8,128)S(1)} %copy-done.34, f32[16,5,256]{2,1,0:T(8,128)} %get-tuple-element.16, f32[16,256]{1,0:T(8,128)S(1)} %copy-done.29, f32[16,5,256]{2,1,0:T(8,128)} %get-tuple-element.15, f32[16,256]{1,0:T(8,128)S(1)} %copy-done.31, ...), kind=kOutput, calls=%fused_computation.38 | convolution fusion | flops 1080164352 | bytes 2146624 | tf_op jit(solution)/shard_map/lspq,mlsq->mlp/dot_general | solution.py:108
  308.7 1.9 collective-permute-start.33
  311.8 3.2 collective-permute-start.34
  315.0 2.2 collective-permute-done.34
  319.1 4.4 %collective-permute-done.35 = f32[16]{0:T(128)S(1)} collective-permute-done((f32[16]{0:T(128)S(1)}, f32[16]{0:T(128)S(1)}, u32[]{:S(2)}, u32[]{:S(2)}) %collective-permute-start.35) | collective-permute-done | bytes 96 | tf_op jit(solution)/shard_map/ppermute | solution.py:38
  323.5 4.3 %collective-permute-start.36 = (f32[16]{0:T(128)S(1)}, f32[16]{0:T(128)S(1)}, u32[]{:S(2)}, u32[]{:S(2)}) collective-permute-start(f32[16]{0:T(128)S(1)} %add.264), channel_id=1, source_target_pairs={{0,8},{1,9},{2,10},{3,11},{4,12},{5,13},{6,14},{7,15},{8,0},{9,1},... | collective-permute-start | bytes 200 | tf_op jit(solution)/shard_map/ppermute | solution.py:38
  327.8 5.0 %collective-permute-done.36 = f32[16]{0:T(128)S(1)} collective-permute-done((f32[16]{0:T(128)S(1)}, f32[16]{0:T(128)S(1)}, u32[]{:S(2)}, u32[]{:S(2)}) %collective-permute-start.36) | collective-permute-done | bytes 96 | tf_op jit(solution)/shard_map/ppermute | solution.py:38
  332.8 5.5 %collective-permute-start.37 = (f32[16]{0:T(128)S(1)}, f32[16]{0:T(128)S(1)}, u32[]{:S(2)}, u32[]{:S(2)}) collective-permute-start(f32[16]{0:T(128)S(1)} %add.265), channel_id=1, source_target_pairs={{0,16},{1,17},{2,18},{3,19},{4,20},{5,21},{6,22},{7,23},{8,24},{9,... | collective-permute-start | bytes 200 | tf_op jit(solution)/shard_map/ppermute | solution.py:38
  338.3 8.6 %collective-permute-done.37 = f32[16]{0:T(128)S(1)} collective-permute-done((f32[16]{0:T(128)S(1)}, f32[16]{0:T(128)S(1)}, u32[]{:S(2)}, u32[]{:S(2)}) %collective-permute-start.37) | collective-permute-done | bytes 96 | tf_op jit(solution)/shard_map/ppermute | solution.py:38
  347.0 3.4 collective-permute-start.38
  350.4 2.0 collective-permute-done.38
  352.4 4.9 %collective-permute-start.39 = (f32[16]{0:T(128)S(1)}, f32[16]{0:T(128)S(1)}, u32[]{:S(2)}, u32[]{:S(2)}) collective-permute-start(f32[16]{0:T(128)S(1)} %add.267), channel_id=1, source_target_pairs={{0,64},{32,96},{64,0},{96,32},{128,192},{160,224},{192,128},{224,1... | collective-permute-start | bytes 200 | tf_op jit(solution)/shard_map/ppermute | solution.py:38
  357.3 2.0 collective-permute-done.39
  359.3 2.2 collective-permute-start.40
  361.5 3.3 collective-permute-done.40
  364.8 4.0 %collective-permute-start.41 = (f32[16]{0:T(128)S(1)}, f32[16]{0:T(128)S(1)}, u32[]{:S(2)}, u32[]{:S(2)}) collective-permute-start(f32[16]{0:T(128)S(1)} %add.269), channel_id=1, source_target_pairs={{0,256},{32,288},{64,320},{96,352},{128,384},{160,416},{192,448},{... | collective-permute-start | bytes 200 | tf_op jit(solution)/shard_map/ppermute | solution.py:38
  368.8 2.9 collective-permute-done.41
  (215 shorter events, 62.8 us)
Async XLA Ops:
  0.6 76.3 %copy-start = (f32[16,4,64,64]{3,2,1,0:T(8,128)S(1)}, f32[16,4,64,64]{3,2,1,0:T(8,128)}, u32[]{:S(2)}) copy-start(f32[16,4,64,64]{3,2,1,0:T(8,128)} %param.15) | copy-start | bytes 3145732
  0.6 26.3 %copy-start.2 = (f32[16,16,256]{2,1,0:T(8,128)S(1)}, f32[16,16,256]{2,1,0:T(8,128)}, u32[]{:S(2)}) copy-start(f32[16,16,256]{2,1,0:T(8,128)} %param.11) | copy-start | bytes 786436
  2.5 30.6 %collective-permute-start = (f32[16]{0:T(128)}, f32[16]{0:T(128)}, u32[]{:S(2)}, u32[]{:S(2)}) collective-permute-start(f32[16]{0:T(128)} %multiply_reduce_fusion.3), channel_id=1, source_target_pairs={{0,1},{1,0},{2,3},{3,2},{4,5},{5,4},{6,7},{7,6},{8,9},{9,8},{10,11... | collective-permute-start | bytes 200 | tf_op jit(solution)/shard_map/ppermute | solution.py:38
  5.8 58.7 %collective-permute-start.11 = (f32[3,2,256]{2,0,1:T(4,128)}, f32[3,2,256]{2,0,1:T(4,128)S(1)}, u32[]{:S(2)}, u32[]{:S(2)}) collective-permute-start(f32[3,2,256]{2,0,1:T(4,128)} %get-tuple-element.21), channel_id=1, source_target_pairs={{0,1},{1,2},{2,3},{3,4},{4,5},{5,6},{6,7},{7,8},{8,9},{9,10},{10,1... | collective-permute-start | bytes 18440 | tf_op jit(solution)/shard_map/ppermute | solution.py:21
  6.3 24.6 %copy-start.38 = (s32[16,4]{0,1:T(4,128)S(1)}, s32[16,4]{0,1:T(4,128)}, u32[]{:S(2)}) copy-start(s32[16,4]{0,1:T(4,128)} %param.19) | copy-start | bytes 772
  6.3 26.1 %copy-start.19 = (f32[3,16,256]{2,1,0:T(8,128)S(1)}, f32[3,16,256]{2,1,0:T(8,128)}, u32[]{:S(2)}) copy-start(f32[3,16,256]{2,1,0:T(8,128)} %param.13) | copy-start | bytes 147460
  6.3 58.2 %collective-permute-start.12 = (f32[3,2,256]{2,0,1:T(4,128)}, f32[3,2,256]{2,0,1:T(4,128)S(1)}, u32[]{:S(2)}, u32[]{:S(2)}) collective-permute-start(f32[3,2,256]{2,0,1:T(4,128)} %get-tuple-element.22), channel_id=1, source_target_pairs={{1,0},{2,1},{3,2},{4,3},{5,4},{6,5},{7,6},{8,7},{9,8},{10,9},{11,1... | collective-permute-start | bytes 18440 | tf_op jit(solution)/shard_map/ppermute | solution.py:23
  19.5 46.8 %all-to-all-start = ((f32[16,1,2048]{2,1,0:T(1,128)}), f32[16,1,2048]{2,1,0:T(1,128)}, u32[]{:S(2)}, u32[]{:S(2)}) async-start(f32[16,1,2048]{2,1,0:T(1,128)} %reshape.113), calls=%async_computation | async-start | bytes 262144 | tf_op jit(solution)/shard_map/all_to_all | solution.py:117
  27.1 42.3 %copy-start.16 = (f32[2,2,64,64]{3,2,1,0:T(8,128)S(1)}, f32[2,2,64,64]{3,2,1,0:T(8,128)}, u32[]{:S(2)}) copy-start(f32[2,2,64,64]{3,2,1,0:T(8,128)} %param.17) | copy-start | bytes 196612
  27.9 43.9 %collective-permute-start.9 = (f32[16,6,320]{2,0,1:T(8,128)}, f32[16,6,320]{2,0,1:T(8,128)}, u32[]{:S(2)}, u32[]{:S(2)}) collective-permute-start(f32[16,6,320]{2,0,1:T(8,128)} %get-tuple-element.17), channel_id=1, source_target_pairs={{0,1},{1,2},{2,3},{3,4},{4,5},{5,6},{6,7},{7,8},{8,9},{9,10},{10,1... | collective-permute-start | bytes 368648 | tf_op jit(solution)/shard_map/ppermute | solution.py:21
  27.9 43.9 %collective-permute-start.10 = (f32[16,6,320]{2,0,1:T(8,128)}, f32[16,6,320]{2,0,1:T(8,128)}, u32[]{:S(2)}, u32[]{:S(2)}) collective-permute-start(f32[16,6,320]{2,0,1:T(8,128)} %get-tuple-element.18), channel_id=1, source_target_pairs={{1,0},{2,1},{3,2},{4,3},{5,4},{6,5},{7,6},{8,7},{9,8},{10,9},{11,1... | collective-permute-start | bytes 368648 | tf_op jit(solution)/shard_map/ppermute | solution.py:23
  33.8 5.4 %collective-permute-start.1 = (f32[16]{0:T(128)S(1)}, f32[16]{0:T(128)S(1)}, u32[]{:S(2)}, u32[]{:S(2)}) collective-permute-start(f32[16]{0:T(128)S(1)} %add.208), channel_id=1, source_target_pairs={{0,2},{1,3},{2,0},{3,1},{4,6},{5,7},{6,4},{7,5},{8,10},{9,11},{10,... | collective-permute-start | bytes 200 | tf_op jit(solution)/shard_map/ppermute | solution.py:38
  39.2 6.3 %collective-permute-start.2 = (f32[16]{0:T(128)S(1)}, f32[16]{0:T(128)S(1)}, u32[]{:S(2)}, u32[]{:S(2)}) collective-permute-start(f32[16]{0:T(128)S(1)} %add.209), channel_id=1, source_target_pairs={{0,4},{1,5},{2,6},{3,7},{4,0},{5,1},{6,2},{7,3},{8,12},{9,13},{10,... | collective-permute-start | bytes 200 | tf_op jit(solution)/shard_map/ppermute | solution.py:38
  45.5 9.3 %collective-permute-start.3 = (f32[16]{0:T(128)S(1)}, f32[16]{0:T(128)S(1)}, u32[]{:S(2)}, u32[]{:S(2)}) collective-permute-start(f32[16]{0:T(128)S(1)} %add.210), channel_id=1, source_target_pairs={{0,8},{1,9},{2,10},{3,11},{4,12},{5,13},{6,14},{7,15},{8,0},{9,1},... | collective-permute-start | bytes 200 | tf_op jit(solution)/shard_map/ppermute | solution.py:38
  55.5 60.5 %collective-permute-start.4 = (f32[16]{0:T(128)}, f32[16]{0:T(128)}, u32[]{:S(2)}, u32[]{:S(2)}) collective-permute-start(f32[16]{0:T(128)} %add.211), channel_id=1, source_target_pairs={{0,16},{1,17},{2,18},{3,19},{4,20},{5,21},{6,22},{7,23},{8,24},{9,... | collective-permute-start | bytes 200 | tf_op jit(solution)/shard_map/ppermute | solution.py:38
  80.9 32.3 %copy-start.1 = (f32[16,256,64]{1,2,0:T(8,128)S(1)}, f32[16,256,64]{1,2,0:T(8,128)}, u32[]{:S(2)}) copy-start(f32[16,256,64]{1,2,0:T(8,128)} %param.14) | copy-start | bytes 3145732
  113.2 70.1 %copy-start.8 = (f32[16,64,64]{2,1,0:T(8,128)S(1)}, f32[16,64,64]{2,1,0:T(8,128)}, u32[]{:S(2)}) copy-start(f32[16,64,64]{2,1,0:T(8,128)} %param.16) | copy-start | bytes 786436
  113.2 73.6 %copy-start.33 = (s32[16]{0:T(128)S(1)}, s32[16]{0:T(128)}, u32[]{:S(2)}) copy-start(s32[16]{0:T(128)} %param.21) | copy-start | bytes 196
  114.0 97.1 %copy-start.10 = (f32[16,16,256]{2,0,1:T(8,128)}, f32[16,16,256]{2,0,1:T(8,128)S(1)}, u32[]{:S(2)}) copy-start(f32[16,16,256]{2,0,1:T(8,128)S(1)} %get-tuple-element.27) | copy-start | bytes 786436
  114.0 3.0 collective-permute-start.13
  117.1 5.4 %collective-permute-start.14 = (f32[16]{0:T(128)S(1)}, f32[16]{0:T(128)S(1)}, u32[]{:S(2)}, u32[]{:S(2)}) collective-permute-start(f32[16]{0:T(128)S(1)} %add.238), channel_id=1, source_target_pairs={{0,2},{1,3},{2,0},{3,1},{4,6},{5,7},{6,4},{7,5},{8,10},{9,11},{10,... | collective-permute-start | bytes 200 | tf_op jit(solution)/shard_map/ppermute | solution.py:38
  119.0 5.4 %collective-permute-start.5 = (f32[16]{0:T(128)S(1)}, f32[16]{0:T(128)S(1)}, u32[]{:S(2)}, u32[]{:S(2)}) collective-permute-start(f32[16]{0:T(128)S(1)} %add.212), channel_id=1, source_target_pairs={{0,32},{32,0},{64,96},{96,64},{128,160},{160,128},{192,224},{224,1... | collective-permute-start | bytes 200 | tf_op jit(solution)/shard_map/ppermute | solution.py:38
  122.5 6.3 %collective-permute-start.15 = (f32[16]{0:T(128)S(1)}, f32[16]{0:T(128)S(1)}, u32[]{:S(2)}, u32[]{:S(2)}) collective-permute-start(f32[16]{0:T(128)S(1)} %add.239), channel_id=1, source_target_pairs={{0,4},{1,5},{2,6},{3,7},{4,0},{5,1},{6,2},{7,3},{8,12},{9,13},{10,... | collective-permute-start | bytes 200 | tf_op jit(solution)/shard_map/ppermute | solution.py:38
  128.8 9.3 %collective-permute-start.16 = (f32[16]{0:T(128)S(1)}, f32[16]{0:T(128)S(1)}, u32[]{:S(2)}, u32[]{:S(2)}) collective-permute-start(f32[16]{0:T(128)S(1)} %add.240), channel_id=1, source_target_pairs={{0,8},{1,9},{2,10},{3,11},{4,12},{5,13},{6,14},{7,15},{8,0},{9,1},... | collective-permute-start | bytes 200 | tf_op jit(solution)/shard_map/ppermute | solution.py:38
  133.1 10.5 %collective-permute-start.6 = (f32[16]{0:T(128)S(1)}, f32[16]{0:T(128)S(1)}, u32[]{:S(2)}, u32[]{:S(2)}) collective-permute-start(f32[16]{0:T(128)S(1)} %add.213), channel_id=1, source_target_pairs={{0,64},{32,96},{64,0},{96,32},{128,192},{160,224},{192,128},{224,1... | collective-permute-start | bytes 200 | tf_op jit(solution)/shard_map/ppermute | solution.py:38
  138.1 14.1 %collective-permute-start.17 = (f32[16]{0:T(128)S(1)}, f32[16]{0:T(128)S(1)}, u32[]{:S(2)}, u32[]{:S(2)}) collective-permute-start(f32[16]{0:T(128)S(1)} %add.241), channel_id=1, source_target_pairs={{0,16},{1,17},{2,18},{3,19},{4,20},{5,21},{6,22},{7,23},{8,24},{9,... | collective-permute-start | bytes 200 | tf_op jit(solution)/shard_map/ppermute | solution.py:38
  152.3 5.9 %collective-permute-start.18 = (f32[16]{0:T(128)S(1)}, f32[16]{0:T(128)S(1)}, u32[]{:S(2)}, u32[]{:S(2)}) collective-permute-start(f32[16]{0:T(128)S(1)} %add.242), channel_id=1, source_target_pairs={{0,32},{32,0},{64,96},{96,64},{128,160},{160,128},{192,224},{224,1... | collective-permute-start | bytes 200 | tf_op jit(solution)/shard_map/ppermute | solution.py:38
  155.7 7.1 %collective-permute-start.7 = (f32[16]{0:T(128)S(1)}, f32[16]{0:T(128)S(1)}, u32[]{:S(2)}, u32[]{:S(2)}) collective-permute-start(f32[16]{0:T(128)S(1)} %add.214), channel_id=1, source_target_pairs={{0,128},{32,160},{64,192},{96,224},{128,0},{160,32},{192,64},{224,... | collective-permute-start | bytes 200 | tf_op jit(solution)/shard_map/ppermute | solution.py:38
  158.2 6.9 %collective-permute-start.19 = (f32[16]{0:T(128)S(1)}, f32[16]{0:T(128)S(1)}, u32[]{:S(2)}, u32[]{:S(2)}) collective-permute-start(f32[16]{0:T(128)S(1)} %add.243), channel_id=1, source_target_pairs={{0,64},{32,96},{64,0},{96,32},{128,192},{160,224},{192,128},{224,1... | collective-permute-start | bytes 200 | tf_op jit(solution)/shard_map/ppermute | solution.py:38
  165.1 7.4 %collective-permute-start.20 = (f32[16]{0:T(128)S(1)}, f32[16]{0:T(128)S(1)}, u32[]{:S(2)}, u32[]{:S(2)}) collective-permute-start(f32[16]{0:T(128)S(1)} %add.244), channel_id=1, source_target_pairs={{0,128},{32,160},{64,192},{96,224},{128,0},{160,32},{192,64},{224,... | collective-permute-start | bytes 200 | tf_op jit(solution)/shard_map/ppermute | solution.py:38
  168.5 7.4 %collective-permute-start.8 = (f32[16]{0:T(128)S(1)}, f32[16]{0:T(128)S(1)}, u32[]{:S(2)}, u32[]{:S(2)}) collective-permute-start(f32[16]{0:T(128)S(1)} %add.215), channel_id=1, source_target_pairs={{0,256},{32,288},{64,320},{96,352},{128,384},{160,416},{192,448},{... | collective-permute-start | bytes 200 | tf_op jit(solution)/shard_map/ppermute | solution.py:38
  172.5 6.9 %collective-permute-start.21 = (f32[16]{0:T(128)S(1)}, f32[16]{0:T(128)S(1)}, u32[]{:S(2)}, u32[]{:S(2)}) collective-permute-start(f32[16]{0:T(128)S(1)} %add.245), channel_id=1, source_target_pairs={{0,256},{32,288},{64,320},{96,352},{128,384},{160,416},{192,448},{... | collective-permute-start | bytes 200 | tf_op jit(solution)/shard_map/ppermute | solution.py:38
  180.2 78.6 %copy-start.5 = (f32[16,16,256]{2,0,1:T(8,128)}, f32[16,16,256]{2,0,1:T(8,128)S(1)}, u32[]{:S(2)}) copy-start(f32[16,16,256]{2,0,1:T(8,128)S(1)} %get-tuple-element.9) | copy-start | bytes 786436
  180.2 3.6 collective-permute-start.22
  183.3 77.0 %copy-start.13 = (f32[16,16,64]{2,0,1:T(8,128)}, f32[16,16,64]{2,0,1:T(8,128)S(1)}, u32[]{:S(2)}) copy-start(f32[16,16,64]{2,0,1:T(8,128)S(1)} %convolution_bitcast_fusion.6) | copy-start | bytes 196612
  183.9 5.4 %collective-permute-start.23 = (f32[16]{0:T(128)S(1)}, f32[16]{0:T(128)S(1)}, u32[]{:S(2)}, u32[]{:S(2)}) collective-permute-start(f32[16]{0:T(128)S(1)} %add.247), channel_id=1, source_target_pairs={{0,2},{1,3},{2,0},{3,1},{4,6},{5,7},{6,4},{7,5},{8,10},{9,11},{10,... | collective-permute-start | bytes 200 | tf_op jit(solution)/shard_map/ppermute | solution.py:38
  189.3 6.3 %collective-permute-start.24 = (f32[16]{0:T(128)S(1)}, f32[16]{0:T(128)S(1)}, u32[]{:S(2)}, u32[]{:S(2)}) collective-permute-start(f32[16]{0:T(128)S(1)} %add.248), channel_id=1, source_target_pairs={{0,4},{1,5},{2,6},{3,7},{4,0},{5,1},{6,2},{7,3},{8,12},{9,13},{10,... | collective-permute-start | bytes 200 | tf_op jit(solution)/shard_map/ppermute | solution.py:38
  195.6 9.3 %collective-permute-start.25 = (f32[16]{0:T(128)S(1)}, f32[16]{0:T(128)S(1)}, u32[]{:S(2)}, u32[]{:S(2)}) collective-permute-start(f32[16]{0:T(128)S(1)} %add.249), channel_id=1, source_target_pairs={{0,8},{1,9},{2,10},{3,11},{4,12},{5,13},{6,14},{7,15},{8,0},{9,1},... | collective-permute-start | bytes 200 | tf_op jit(solution)/shard_map/ppermute | solution.py:38
  205.0 14.1 %collective-permute-start.26 = (f32[16]{0:T(128)S(1)}, f32[16]{0:T(128)S(1)}, u32[]{:S(2)}, u32[]{:S(2)}) collective-permute-start(f32[16]{0:T(128)S(1)} %add.250), channel_id=1, source_target_pairs={{0,16},{1,17},{2,18},{3,19},{4,20},{5,21},{6,22},{7,23},{8,24},{9,... | collective-permute-start | bytes 200 | tf_op jit(solution)/shard_map/ppermute | solution.py:38
  219.6 5.7 %collective-permute-start.27 = (f32[16]{0:T(128)}, f32[16]{0:T(128)}, u32[]{:S(2)}, u32[]{:S(2)}) collective-permute-start(f32[16]{0:T(128)} %add.251), channel_id=1, source_target_pairs={{0,32},{32,0},{64,96},{96,64},{128,160},{160,128},{192,224},{224,1... | collective-permute-start | bytes 200 | tf_op jit(solution)/shard_map/ppermute | solution.py:38
  226.5 10.0 %collective-permute-start.28 = (f32[16]{0:T(128)}, f32[16]{0:T(128)}, u32[]{:S(2)}, u32[]{:S(2)}) collective-permute-start(f32[16]{0:T(128)} %add.252), channel_id=1, source_target_pairs={{0,64},{32,96},{64,0},{96,32},{128,192},{160,224},{192,128},{224,1... | collective-permute-start | bytes 200 | tf_op jit(solution)/shard_map/ppermute | solution.py:38
  231.1 19.5 %all-to-all-start.1 = ((f32[16,1,2048]{2,1,0:T(1,128)}), f32[16,1,2048]{2,1,0:T(1,128)}, u32[]{:S(2)}, u32[]{:S(2)}) async-start(f32[16,1,2048]{2,1,0:T(1,128)} %reshape.115), calls=%async_computation.1 | async-start | bytes 262144 | tf_op jit(solution)/shard_map/all_to_all | solution.py:117
  237.1 5.4 %collective-permute-start.29 = (f32[16]{0:T(128)S(1)}, f32[16]{0:T(128)S(1)}, u32[]{:S(2)}, u32[]{:S(2)}) collective-permute-start(f32[16]{0:T(128)S(1)} %add.253), channel_id=1, source_target_pairs={{0,128},{32,160},{64,192},{96,224},{128,0},{160,32},{192,64},{224,... | collective-permute-start | bytes 200 | tf_op jit(solution)/shard_map/ppermute | solution.py:38
  239.2 19.5 %collective-permute-start.31 = (f32[16,6,320]{2,0,1:T(8,128)}, f32[16,6,320]{2,0,1:T(8,128)}, u32[]{:S(2)}, u32[]{:S(2)}) collective-permute-start(f32[16,6,320]{2,0,1:T(8,128)} %get-tuple-element.12), channel_id=1, source_target_pairs={{0,1},{1,2},{2,3},{3,4},{4,5},{5,6},{6,7},{7,8},{8,9},{9,10},{10,1... | collective-permute-start | bytes 368648 | tf_op jit(solution)/shard_map/ppermute | solution.py:21
  242.5 6.9 %collective-permute-start.30 = (f32[16]{0:T(128)S(1)}, f32[16]{0:T(128)S(1)}, u32[]{:S(2)}, u32[]{:S(2)}) collective-permute-start(f32[16]{0:T(128)S(1)} %add.254), channel_id=1, source_target_pairs={{0,256},{32,288},{64,320},{96,352},{128,384},{160,416},{192,448},{... | collective-permute-start | bytes 200 | tf_op jit(solution)/shard_map/ppermute | solution.py:38
  246.5 12.2 %collective-permute-start.32 = (f32[16,6,320]{2,0,1:T(8,128)}, f32[16,6,320]{2,0,1:T(8,128)}, u32[]{:S(2)}, u32[]{:S(2)}) collective-permute-start(f32[16,6,320]{2,0,1:T(8,128)} %get-tuple-element.13), channel_id=1, source_target_pairs={{1,0},{2,1},{3,2},{4,3},{5,4},{6,5},{7,6},{8,7},{9,8},{10,9},{11,1... | collective-permute-start | bytes 368648 | tf_op jit(solution)/shard_map/ppermute | solution.py:23
  272.4 34.5 %copy-start.9 = (f32[16,64,64]{2,1,0:T(8,128)S(1)}, f32[16,64,64]{2,1,0:T(8,128)}, u32[]{:S(2)}) copy-start(f32[16,64,64]{2,1,0:T(8,128)} %param.16) | copy-start | bytes 786436
  272.4 34.5 %copy-start.15 = (f32[16,16,64]{2,0,1:T(8,128)S(1)}, f32[16,16,64]{2,0,1:T(8,128)}, u32[]{:S(2)}) copy-start(f32[16,16,64]{2,0,1:T(8,128)} %copy.55) | copy-start | bytes 196612
  272.4 34.5 %copy-start.17 = (f32[16,16,64]{2,1,0:T(8,128)S(1)}, f32[16,16,64]{2,1,0:T(8,128)}, u32[]{:S(2)}) copy-start(f32[16,16,64]{2,1,0:T(8,128)} %convolution_bitcast_fusion.4) | copy-start | bytes 196612
  272.4 35.5 %copy-start.4 = (f32[16,16,256]{2,1,0:T(8,128)S(1)}, f32[16,16,256]{2,1,0:T(8,128)}, u32[]{:S(2)}) copy-start(f32[16,16,256]{2,1,0:T(8,128)} %param.11) | copy-start | bytes 786436
  272.4 35.5 %copy-start.6 = (f32[16,16,256]{2,0,1:T(8,128)S(1)}, f32[16,16,256]{2,0,1:T(8,128)}, u32[]{:S(2)}) copy-start(f32[16,16,256]{2,0,1:T(8,128)} %copy-done.5) | copy-start | bytes 786436
  272.4 35.5 %copy-start.11 = (f32[16,16,256]{2,0,1:T(8,128)S(1)}, f32[16,16,256]{2,0,1:T(8,128)}, u32[]{:S(2)}) copy-start(f32[16,16,256]{2,0,1:T(8,128)} %copy-done.10) | copy-start | bytes 786436
  272.4 35.5 %copy-start.35 = (f32[16]{0:T(128)S(1)}, f32[16]{0:T(128)}, u32[]{:S(2)}) copy-start(f32[16]{0:T(128)} %get-tuple-element.6) | copy-start | bytes 196
  306.9 64.8 %copy-start.39 = (f32[16]{0:T(128)S(1)}, f32[16]{0:T(128)}, u32[]{:S(2)}) copy-start(f32[16]{0:T(128)} %get-tuple-element.7) | copy-start | bytes 196
  306.9 64.8 %copy-start.37 = (f32[16]{0:T(128)S(1)}, f32[16]{0:T(128)}, u32[]{:S(2)}) copy-start(f32[16]{0:T(128)} %copy-done.36) | copy-start | bytes 196
  308.7 3.0 collective-permute-start.33
  311.8 5.4 %collective-permute-start.34 = (f32[16]{0:T(128)S(1)}, f32[16]{0:T(128)S(1)}, u32[]{:S(2)}, u32[]{:S(2)}) collective-permute-start(f32[16]{0:T(128)S(1)} %add.262), channel_id=1, source_target_pairs={{0,2},{1,3},{2,0},{3,1},{4,6},{5,7},{6,4},{7,5},{8,10},{9,11},{10,... | collective-permute-start | bytes 200 | tf_op jit(solution)/shard_map/ppermute | solution.py:38
  317.2 6.3 %collective-permute-start.35 = (f32[16]{0:T(128)S(1)}, f32[16]{0:T(128)S(1)}, u32[]{:S(2)}, u32[]{:S(2)}) collective-permute-start(f32[16]{0:T(128)S(1)} %add.263), channel_id=1, source_target_pairs={{0,4},{1,5},{2,6},{3,7},{4,0},{5,1},{6,2},{7,3},{8,12},{9,13},{10,... | collective-permute-start | bytes 200 | tf_op jit(solution)/shard_map/ppermute | solution.py:38
  323.5 9.3 %collective-permute-start.36 = (f32[16]{0:T(128)S(1)}, f32[16]{0:T(128)S(1)}, u32[]{:S(2)}, u32[]{:S(2)}) collective-permute-start(f32[16]{0:T(128)S(1)} %add.264), channel_id=1, source_target_pairs={{0,8},{1,9},{2,10},{3,11},{4,12},{5,13},{6,14},{7,15},{8,0},{9,1},... | collective-permute-start | bytes 200 | tf_op jit(solution)/shard_map/ppermute | solution.py:38
  332.8 14.1 %collective-permute-start.37 = (f32[16]{0:T(128)S(1)}, f32[16]{0:T(128)S(1)}, u32[]{:S(2)}, u32[]{:S(2)}) collective-permute-start(f32[16]{0:T(128)S(1)} %add.265), channel_id=1, source_target_pairs={{0,16},{1,17},{2,18},{3,19},{4,20},{5,21},{6,22},{7,23},{8,24},{9,... | collective-permute-start | bytes 200 | tf_op jit(solution)/shard_map/ppermute | solution.py:38
  347.0 5.4 %collective-permute-start.38 = (f32[16]{0:T(128)S(1)}, f32[16]{0:T(128)S(1)}, u32[]{:S(2)}, u32[]{:S(2)}) collective-permute-start(f32[16]{0:T(128)S(1)} %add.266), channel_id=1, source_target_pairs={{0,32},{32,0},{64,96},{96,64},{128,160},{160,128},{192,224},{224,1... | collective-permute-start | bytes 200 | tf_op jit(solution)/shard_map/ppermute | solution.py:38
  352.4 6.9 %collective-permute-start.39 = (f32[16]{0:T(128)S(1)}, f32[16]{0:T(128)S(1)}, u32[]{:S(2)}, u32[]{:S(2)}) collective-permute-start(f32[16]{0:T(128)S(1)} %add.267), channel_id=1, source_target_pairs={{0,64},{32,96},{64,0},{96,32},{128,192},{160,224},{192,128},{224,1... | collective-permute-start | bytes 200 | tf_op jit(solution)/shard_map/ppermute | solution.py:38
  359.3 5.4 %collective-permute-start.40 = (f32[16]{0:T(128)S(1)}, f32[16]{0:T(128)S(1)}, u32[]{:S(2)}, u32[]{:S(2)}) collective-permute-start(f32[16]{0:T(128)S(1)} %add.268), channel_id=1, source_target_pairs={{0,128},{32,160},{64,192},{96,224},{128,0},{160,32},{192,64},{224,... | collective-permute-start | bytes 200 | tf_op jit(solution)/shard_map/ppermute | solution.py:38
  364.8 6.9 %collective-permute-start.41 = (f32[16]{0:T(128)S(1)}, f32[16]{0:T(128)S(1)}, u32[]{:S(2)}, u32[]{:S(2)}) collective-permute-start(f32[16]{0:T(128)S(1)} %add.269), channel_id=1, source_target_pairs={{0,256},{32,288},{64,320},{96,352},{128,384},{160,416},{192,448},{... | collective-permute-start | bytes 200 | tf_op jit(solution)/shard_map/ppermute | solution.py:38
  (23 other events, 154.6 us)
